TPU v7x, 256 devices: a whole 4x4x8 slice. The times are simulated.
256 devices in a mesh: segment: 4 (over z_lo), expert: 64 (over x, y, z_hi, core).
Axes of the slice: x: 4, y: 4, z: 8 (z_hi: 2, z_lo: 4; z = z_hi * 4 + z_lo), core: 2. Of those that a mesh axis runs over, the one named last changes fastest.
Arguments:
- forward_input: bfloat16 [4, 512, 7168], P('segment', 'expert'), may hold values from -6 to 6
- forward_routes: int32 [4, 512, 8], P('segment', 'expert'), may hold values from 0 to 15, all different within a row; in each aligned block of 8 rows (0 to 7, 8 to 15, ..., all dimensions but the last counted through in order) at most 8 rows name the same one
- forward_gates: float32 [4, 512, 8], P('segment', 'expert'), may hold values from 0.05 to 0.8
- gate_matrix: bfloat16 [4, 64, 7168, 256], P('segment', 'expert'), may hold values from -0.0625 to 0.0625
- up_matrix: bfloat16 [4, 64, 7168, 256], P('segment', 'expert'), may hold values from -0.0625 to 0.0625
- down_matrix: bfloat16 [4, 64, 256, 7168], P('segment', 'expert'), may hold values from -0.1875 to 0.1875
Outputs:
- next_input: bfloat16 [4, 512, 7168], P('segment', 'expert')
Inputs may be any that keep to these rules, and one draw needn't show every extreme that they name: `forward_routes`: each token names 8 different experts. Among the 8 tokens of one index of expert, no expert is named by more than 8 of them, and in every draw some expert is named by exactly 8 tokens of some index.
All inputs are finite; a program needn't handle non-finite values.
Results may differ from a plain program's by a relative error of at most 0.0065.
Values may be sent and summed in bfloat16 or wider, within the bound.
No kernel may reach another device: no remote copies, remote signals or barrier semaphores. Data moves between devices by JAX's collectives and lax.ppermute only.
A program may use at most 128 MiB of HBM per device.

v0:
```python
import jax
import jax.numpy as jnp
from jax import lax
from jax.sharding import PartitionSpec as P

FH = 1024


def passed_along(value, axis, steps):
    count = lax.axis_size(axis)
    pairs = [(source, (source + steps) % count) for source in range(count)]
    return lax.ppermute(value, axis, pairs)


def local(forward_input, forward_routes, forward_gates, gate_matrix, up_matrix, down_matrix):
    devices = lax.axis_size("expert")
    hidden_slice = gate_matrix.shape[3]
    split = FH // hidden_slice
    groups = devices // split
    tokens = forward_input[0]
    me = lax.axis_index("expert")
    expert = me % groups
    rows = lax.all_gather(tokens, "expert", axis=0, tiled=True)
    routes = lax.all_gather(forward_routes[0], "expert", axis=0, tiled=True)
    gates = lax.all_gather(forward_gates[0], "expert", axis=0, tiled=True)
    weight = jnp.sum(jnp.where(routes == expert, gates, 0.0), axis=1)
    gate_act = jnp.dot(rows, gate_matrix[0, 0], preferred_element_type=jnp.float32)
    upper_act = jnp.dot(rows, up_matrix[0, 0], preferred_element_type=jnp.float32)
    hidden = (jax.nn.silu(gate_act) * upper_act).astype(jnp.bfloat16)
    partial = jnp.dot(hidden, down_matrix[0, 0], preferred_element_type=jnp.float32)
    partial = partial.astype(jnp.bfloat16).astype(jnp.float32)
    weighted = (weight[:, None] * partial).astype(jnp.bfloat16)
    mixed = lax.psum_scatter(weighted, "expert", scatter_dimension=0, tiled=True)
    layer_out = (tokens.astype(jnp.float32) + mixed.astype(jnp.float32)).astype(jnp.bfloat16)
    next_input = passed_along(layer_out, "segment", 1)
    return next_input[None]


def solution(mesh):
    in_specs = (
        P("segment", "expert", None),
        P("segment", "expert", None),
        P("segment", "expert", None),
        P("segment", "expert", None, None),
        P("segment", "expert", None, None),
        P("segment", "expert", None, None),
    )
    out_specs = P("segment", "expert", None)
    return jax.shard_map(local, mesh=mesh, in_specs=in_specs, out_specs=out_specs, check_vma=False)
```

profile of v0, /device:TPU:0, one launch (start us, length us, event | category | flops | bytes accessed | tf_op | source)
XLA Modules:
  0.0 718.2 jit_solution(15679720350931443463)
XLA Ops:
  6.5 0.0 all-gather.5.cloned.1.call-start
  6.5 0.7 all-gather.5.cloned.1.call-update
  7.3 0.0 reduce-scatter.2.cloned.1.call-start
  7.3 125.8 %all-gather = s32[1,512,8]{2,1,0:T(8,128)S(1)} all-gather(s32[1,8,8]{2,1,0:T(8,128)} %param.7), channel_id=2, replica_groups=mesh['segment'=4,'expert'=64] {'expert'}, dimensions={1}, use_global_device_ids=true | all-gather | bytes 16640 | tf_op jit(solution)/shard_map/all_gather | solution.py:24
  133.1 109.0 %all-gather.1 = f32[1,512,8]{2,1,0:T(8,128)S(1)} all-gather(f32[1,8,8]{2,1,0:T(8,128)} %param.8), channel_id=3, replica_groups=mesh['segment'=4,'expert'=64] {'expert'}, dimensions={1}, use_global_device_ids=true | all-gather | bytes 16640 | tf_op jit(solution)/shard_map/all_gather | solution.py:25
  242.1 0.1 select_reduce_fusion
  242.2 0.0 all-gather.5.cloned.1.call-done
  242.2 6.2 fusion.2
  248.4 15.9 %multiply_convert_fusion = bf16[512,7168]{1,0:T(8,128)(2,1)} fusion(f32[512]{0:T(512)S(1)} %select_reduce_fusion, bf16[1,1,256,7168]{3,2,1,0:T(8,128)(2,1)} %param.11, bf16[1,1,7168,256]{3,2,1,0:T(8,128)(2,1)} %param.10, bf16[1,512,7168]{2,1,0:T(8,128)(2,1)} %all-gather.5.cloned.1.call-done, f32[512,256]{1,0:T(8,128)S(1)} %fusion.2), kind=kOutput, calls=%fused_computation | convolution fusion | flops 3773562880 | bytes 22546432 | tf_op jit(solution)/shard_map/dot_general | solution.py:30
  264.4 0.0 copy-start
  264.4 0.0 reduce-scatter.2.cloned.1.call-update
  264.4 438.7 %reduce-scatter.2.cloned.1.call-done = bf16[8,7168]{1,0:T(8,128)(2,1)} async-done(((bf16[512,7168]{1,0:T(8,128)(2,1)}), bf16[8,7168]{1,0:T(8,128)(2,1)}) %reduce-scatter.2.cloned.1.call-update) | async-done | bytes 114704 | tf_op jit(solution)/shard_map/reduce_scatter | solution.py:33
  703.1 0.0 copy-done
  703.1 0.9 fusion.17
  704.0 0.1 collective-permute-start
  704.1 6.6 collective-permute-done
  710.7 0.6 copy.8
Async XLA Ops:
  6.5 235.7 %all-gather.5.cloned.1.call-start = ((), (), s32[]{:S(2)}) async-start(), calls=%async_computation.2 | async-start | bytes 7454720 | tf_op jit(solution)/shard_map/all_gather | solution.py:23
  7.3 695.9 %reduce-scatter.2.cloned.1.call-start = ((), (), s32[]{:S(2)}) async-start(), calls=%async_computation.1 | async-start | bytes 7454720 | tf_op jit(solution)/shard_map/reduce_scatter | solution.py:33
  264.4 438.7 %copy-start = (bf16[1,8,7168]{2,1,0:T(8,128)(2,1)S(1)}, bf16[1,8,7168]{2,1,0:T(8,128)(2,1)}, u32[]{:S(2)}) copy-start(bf16[1,8,7168]{2,1,0:T(8,128)(2,1)} %param.6) | copy-start | bytes 344068
  704.0 6.7 collective-permute-start
Sparse Core Ops, SparseCore 0:
  10.8 110.3 all-gather.4
  264.5 438.5 reduce-scatter.1
where the time goes:
time: 718 us
  waiting for transfers between devices  446 us (62%)
  blocking collectives  235 us (33%)
  matrix products  22.1 us (3%)
  between operations  13.4 us (2%)
    reduce_scatter x1, waiting for transfers between devices, local(): lax.psum_scatter(weighted, 'expert', scatter_dimension=0, tiled=True)  439 us
    all_gather x1, blocking collectives, local(): routes = lax.all_gather(forward_routes[0], 'expert', axis=0, tiled=True)  126 us
    all_gather x1, blocking collectives, local(): gates = lax.all_gather(forward_gates[0], 'expert', axis=0, tiled=True)  109 us
    dot_general x1, matrix products, local(): jnp.dot(hidden, down_matrix[0, 0], preferred_element_type=jnp.float32)  15.9 us
  transfers between devices with their start and end apart: 3, of which 2 were waited for; matrix products, arithmetic and copies ran while one was open for 0% of the time, Pallas kernels for 0%

commit v1 on v0

--- a/solution.py
+++ b/solution.py
@@ -22,7 +22,10 @@
     expert = me % groups
     rows = lax.all_gather(tokens, "expert", axis=0, tiled=True)
     routes = lax.all_gather(forward_routes[0], "expert", axis=0, tiled=True)
-    gates = lax.all_gather(forward_gates[0], "expert", axis=0, tiled=True)
+    gates = jnp.concatenate(
+        lax.all_to_all(jnp.stack([forward_gates[0]] * lax.axis_size("expert")), "expert", 0, 0),
+        axis=0,
+    )
     weight = jnp.sum(jnp.where(routes == expert, gates, 0.0), axis=1)
     gate_act = jnp.dot(rows, gate_matrix[0, 0], preferred_element_type=jnp.float32)
     upper_act = jnp.dot(rows, up_matrix[0, 0], preferred_element_type=jnp.float32)

time: 718 us -> 615 us (0.86)
  blocking collectives: 235 us -> 122 us
  starting transfers between devices: 0.12 us -> 14 us
    all_gather x1 -> x0, blocking collectives: 109 us -> none  [local(): gates = lax.all_gather(forward_gates[0], 'expert', axis=0, tiled=True)]
    all_to_all x0 -> x1, starting transfers between devices: none -> 12.9 us  [local(): lax.all_to_all(jnp.stack([forward_gates[0]] * lax.axis_size('expert')), '...]
  transfers between devices with their start and end apart: 3 -> 4, of which waited for: 2 -> 2; matrix products, arithmetic and copies ran while one was open for 0% -> 0% of each run, Pallas kernels for 0% -> 0%
where the time goes in v1:
time: 615 us
  waiting for transfers between devices  440 us (72%)
  blocking collectives  122 us (20%)
  matrix products  22.2 us (4%)
  starting transfers between devices  14 us (2%)
  between operations  13.4 us (2%)
    reduce_scatter x1, waiting for transfers between devices, local(): lax.psum_scatter(weighted, 'expert', scatter_dimension=0, tiled=True)  433 us
    all_gather x1, blocking collectives, local(): routes = lax.all_gather(forward_routes[0], 'expert', axis=0, tiled=True)  122 us
    dot_general x1, matrix products, local(): jnp.dot(hidden, down_matrix[0, 0], preferred_element_type=jnp.float32)  16 us
    all_to_all x1, starting transfers between devices, local(): lax.all_to_all(jnp.stack([forward_gates[0]] * lax.axis_size('expert')), '...  12.9 us
  transfers between devices with their start and end apart: 4, of which 2 were waited for; matrix products, arithmetic and copies ran while one was open for 0% of the time, Pallas kernels for 0%

profile of v1, /device:TPU:0, one launch (start us, length us, event | category | flops | bytes accessed | tf_op | source)
XLA Modules:
  0.0 614.6 jit_solution(10083953702663133053)
XLA Ops:
  6.5 0.0 all-gather.4.cloned.1.call-start
  6.5 0.7 all-gather.4.cloned.1.call-update
  7.3 1.4 stack.3
  8.7 12.9 %all-to-all-start = ((f32[64,8,8]{2,1,0:T(8,128)}), f32[64,8,8]{2,1,0:T(8,128)S(1)}, u32[]{:S(2)}, u32[]{:S(2)}) async-start(f32[64,8,8]{2,1,0:T(8,128)} %stack.3), calls=%async_computation | async-start | bytes 524288 | tf_op jit(solution)/shard_map/all_to_all | solution.py:26
  21.5 0.0 reduce-scatter.2.cloned.1.call-start
  21.6 122.2 %all-gather = s32[1,512,8]{2,1,0:T(8,128)S(1)} all-gather(s32[1,8,8]{2,1,0:T(8,128)} %param.7), channel_id=2, replica_groups=mesh['segment'=4,'expert'=64] {'expert'}, dimensions={1}, use_global_device_ids=true | all-gather | bytes 16640 | tf_op jit(solution)/shard_map/all_gather | solution.py:24
  143.8 0.0 all-to-all-done
  143.8 0.2 fusion.17
  144.0 0.0 all-gather.4.cloned.1.call-done
  144.0 6.2 %fusion.2 = f32[512,256]{1,0:T(8,128)S(1)} fusion(bf16[1,512,7168]{2,1,0:T(8,128)(2,1)} %all-gather.4.cloned.1.call-done, bf16[1,1,7168,256]{3,2,1,0:T(8,128)(2,1)} %param.9), kind=kOutput, calls=%fused_computation.4 | convolution fusion | flops 1879048192 | bytes 11534336 | tf_op jit(solution)/shard_map/dot_general | solution.py:30
  150.2 16.0 %multiply_convert_fusion = bf16[512,7168]{1,0:T(8,128)(2,1)} fusion(f32[512]{0:T(512)S(1)} %fusion.17, bf16[1,1,256,7168]{3,2,1,0:T(8,128)(2,1)} %param.11, bf16[1,1,7168,256]{3,2,1,0:T(8,128)(2,1)} %param.10, bf16[1,512,7168]{2,1,0:T(8,128)(2,1)} %all-gather.4.cloned.1.call-done, f32[512,256]{1,0:T(8,128)S(1)} %fusion.2), kind=kOutput, calls=%fused_computation | convolution fusion | flops 3773562880 | bytes 22546432 | tf_op jit(solution)/shard_map/dot_general | solution.py:33
  166.2 0.0 copy-start
  166.2 0.0 reduce-scatter.2.cloned.1.call-update
  166.2 433.3 %reduce-scatter.2.cloned.1.call-done = bf16[8,7168]{1,0:T(8,128)(2,1)} async-done(((bf16[512,7168]{1,0:T(8,128)(2,1)}), bf16[8,7168]{1,0:T(8,128)(2,1)}) %reduce-scatter.2.cloned.1.call-update) | async-done | bytes 114704 | tf_op jit(solution)/shard_map/reduce_scatter | solution.py:36
  599.6 0.0 copy-done
  599.6 0.9 fusion.18
  600.5 1.1 collective-permute-start
  601.6 5.6 collective-permute-done
  607.2 0.6 copy.8
Async XLA Ops:
  6.5 137.5 %all-gather.4.cloned.1.call-start = ((), (), s32[]{:S(2)}) async-start(), calls=%async_computation.3 | async-start | bytes 7454720 | tf_op jit(solution)/shard_map/all_gather | solution.py:23
  8.7 135.1 %all-to-all-start = ((f32[64,8,8]{2,1,0:T(8,128)}), f32[64,8,8]{2,1,0:T(8,128)S(1)}, u32[]{:S(2)}, u32[]{:S(2)}) async-start(f32[64,8,8]{2,1,0:T(8,128)} %stack.3), calls=%async_computation | async-start | bytes 524288 | tf_op jit(solution)/shard_map/all_to_all | solution.py:26
  21.5 578.0 %reduce-scatter.2.cloned.1.call-start = ((), (), s32[]{:S(2)}) async-start(), calls=%async_computation.2 | async-start | bytes 7454720 | tf_op jit(solution)/shard_map/reduce_scatter | solution.py:36
  166.2 433.4 %copy-start = (bf16[1,8,7168]{2,1,0:T(8,128)(2,1)S(1)}, bf16[1,8,7168]{2,1,0:T(8,128)(2,1)}, u32[]{:S(2)}) copy-start(bf16[1,8,7168]{2,1,0:T(8,128)(2,1)} %param.6) | copy-start | bytes 344068
  600.5 6.7 %collective-permute-start = (bf16[8,7168]{1,0:T(8,128)(2,1)S(1)}, bf16[8,7168]{1,0:T(8,128)(2,1)S(1)}, u32[]{:S(2)}, u32[]{:S(2)}) collective-permute-start(bf16[8,7168]{1,0:T(8,128)(2,1)S(1)} %fusion.18), channel_id=1, source_target_pairs={{0,64},{64,128},{128,192},{192,0},{1,65},{65,129},{129,193},{193,1... | collective-permute-start | bytes 344072 | tf_op jit(solution)/shard_map/ppermute | solution.py:12
Sparse Core Ops, SparseCore 0:
  10.8 111.5 all-gather.3
  166.3 433.1 reduce-scatter.1
